TPU v7x, 512 devices: a whole 4x8x8 slice. The times are simulated.
512 devices in a mesh: band: 32 (over x, y), seq: 16 (over z, core).
Axes of the slice: x: 4, y: 8, z: 8, core: 2. Of those that a mesh axis runs over, the one named last changes fastest.
Arguments:
- posteriors: bfloat16 [32, 262144], P(None, ('band', 'seq'))
- seed_mask: int32 [262144], P(('band', 'seq')), may hold values 0 or 1
- frame_perm: int32 [512, 512], P(('band', 'seq')), may hold values from 0 to 511, each once within a row
- lengths: int32 [256], replicated, may hold values from 1 to 4096, 262144 in all
- embeddings: bfloat16 [262144, 256], P(('band', 'seq')), may hold values from -12 to 12
- partners: int32 [2048, 32], P(('band', 'seq')), may hold values from 0 to 127, as said below
- levels: int32 [2048, 32], P(('band', 'seq')), may hold values from 1 to 8, as said below
Outputs:
- spread_labels: float32 [32, 262144], P(None, ('band', 'seq'))
Inputs may be any that keep to these rules, and one draw needn't show every extreme that they name: `partners`: within each seq index s, slot k pairs the 128 tiles mutually: if tile number a names b in slot k then b names a in slot k; no tile names itself. `levels`: two tiles paired in slot k carry the same level.
All inputs are finite; a program needn't handle non-finite values. No bound on the sum of `seed_mask` on one device may be relied on, other than what follows from the above.
Results may differ from a plain program's by a relative error of at most 0.007.
Values may be sent and summed in bfloat16 or wider, within the bound.
No kernel may reach another device: no remote copies, remote signals or barrier semaphores. Data moves between devices by JAX's collectives and lax.ppermute only.
A program may use at most 64 MiB of HBM per device.

v0:
```python
import math
import jax
import jax.numpy as jnp
from jax import lax
from jax.sharding import PartitionSpec as P

RADIUS = 64
ITERS = 3
decay_len = 16.0
spread_rate = 0.9


def with_halo(cells, sides, width):
    for axis, dim in sides:
        count = lax.axis_size(axis)
        ends = count - 1
        head = lax.slice_in_dim(cells, 0, width, axis=dim)
        tail = lax.slice_in_dim(cells, cells.shape[dim] - width, cells.shape[dim], axis=dim)
        cells = jnp.concatenate(
            [
                lax.ppermute(tail, axis, [(i, (i + 1) % count) for i in range(ends)]),
                cells,
                lax.ppermute(head, axis, [((i + 1) % count, i) for i in range(ends)]),
            ],
            axis=dim,
        )
    return cells


def on_device(posteriors, seed_mask, frame_perm, lengths, embeddings, partners, levels):
    channels, frames = posteriors.shape
    band_count = lax.axis_size("band")
    groups = lax.axis_size("seq")
    tile_count = frames // 128
    seeded = posteriors * seed_mask.astype(jnp.bfloat16)[None, :]
    ordered = jnp.take(seeded, frame_perm[0], axis=1).reshape(
        channels, band_count, frames // band_count
    )
    arrived = lax.all_to_all(ordered, "band", split_axis=1, concat_axis=1, tiled=True)
    labels = arrived.reshape(channels, frames).astype(jnp.float32)
    device = lax.axis_index("band") * groups + lax.axis_index("seq")
    frame_total = frames * band_count * groups
    window = 128 + 2 * RADIUS
    global_at = device * frames - RADIUS + jnp.arange(frames + 2 * RADIUS, dtype=jnp.int32)
    utt_ends = jnp.cumsum(lengths)
    owner_seg = jnp.sum((utt_ends[None, :] <= global_at[:, None]).astype(jnp.int32), axis=1)
    inside = (global_at >= 0) & (global_at < frame_total)
    tile_off = (jnp.arange(tile_count, dtype=jnp.int32) * 128)[:, None, None]
    win_pos = tile_off + jnp.arange(window, dtype=jnp.int32)[None, :, None]
    row_pos = tile_off + RADIUS + jnp.arange(128, dtype=jnp.int32)[None, None, :]
    offset = jnp.abs(win_pos - row_pos)
    linked = (
        (offset >= 1)
        & (offset <= RADIUS)
        & (owner_seg[win_pos] == owner_seg[row_pos])
        & inside[win_pos]
    )
    band_tiles = jnp.where(
        linked, jnp.exp(-offset.astype(jnp.float32) / decay_len), jnp.float32(0.0)
    ).astype(jnp.bfloat16)
    near_degree = jnp.sum(band_tiles.astype(jnp.float32), axis=1).reshape(frames)
    gathered = lax.all_gather(embeddings, "band", axis=0, tiled=True)
    embed_width = embeddings.shape[1]
    partner_rows = gathered.reshape(-1, 128, embed_width)[partners]
    own_rows = embeddings.reshape(tile_count, 128, embed_width)
    inner_prod = jnp.einsum(
        "tkje,tie->tkji", partner_rows, own_rows, preferred_element_type=jnp.float32
    )
    affinity = (
        jnp.exp(0.5 * (inner_prod / math.sqrt(embed_width)))
        * (levels.astype(jnp.float32) / 8.0)[:, :, None, None]
        / 128.0
    )
    affinity = affinity.astype(jnp.bfloat16)
    far_degree = jnp.sum(affinity.astype(jnp.float32), axis=(1, 2)).reshape(frames)
    norm_scale = 1.0 / jnp.sqrt(near_degree + far_degree)

    def squares(residual):
        return lax.psum(jnp.sum(residual * residual, axis=1), ("band", "seq"))

    solution = jnp.zeros((channels, frames), jnp.float32)
    residual = labels
    direction = labels
    norm_now = squares(residual)
    for iteration in range(ITERS):
        lifted = (norm_scale[None, :] * direction).astype(jnp.bfloat16)
        padded = with_halo(lifted, ((("band", "seq"), 1),), RADIUS)
        windows = jnp.stack(
            [padded[:, position * 128 : position * 128 + window] for position in range(tile_count)],
            axis=0,
        )
        near_term = jnp.einsum(
            "tcw,twa->cta", windows, band_tiles, preferred_element_type=jnp.float32
        ).reshape(channels, frames)
        spread = lax.all_gather(lifted, "band", axis=1, tiled=True).reshape(channels, -1, 128)
        far_tiles = spread[:, partners]
        far_term = jnp.einsum(
            "ctkj,tkji->cti", far_tiles, affinity, preferred_element_type=jnp.float32
        ).reshape(channels, frames)
        image = direction - spread_rate * norm_scale[None, :] * (near_term + far_term)
        curve = lax.psum(jnp.sum(direction * image, axis=1), ("band", "seq"))
        alpha = norm_now / curve
        solution = solution + alpha[:, None] * direction
        residual = residual - alpha[:, None] * image
        norm_next = squares(residual)
        direction = residual + (norm_next / norm_now)[:, None] * direction
        norm_now = norm_next
    return solution


def solution(mesh):
    placed = (
        P(None, ("band", "seq")),
        P(("band", "seq")),
        P(("band", "seq"), None),
        P(),
        P(("band", "seq"), None),
        P(("band", "seq"), None),
        P(("band", "seq"), None),
    )
    return jax.shard_map(
        on_device, mesh=mesh, in_specs=placed, out_specs=P(None, ("band", "seq")), check_vma=False
    )
```

profile of v0, /device:TPU:1, one launch (start us, length us, event | category | flops | bytes accessed | tf_op | source)
XLA Modules:
  0.0 862.8 jit_solution(14141777168958132764)
XLA Ops:
  6.5 0.7 all-gather.5.cloned.1.call-update
  7.3 0.7 convert_element_type.47
  7.9 0.8 broadcast_multiply_fusion
  8.8 0.5 broadcast.328
  9.4 1.3 reduce.11
  10.8 0.7 compare_select_fusion.1
  11.5 1.3 gather_fusion
  12.8 0.1 fusion.73
  13.0 0.8 reshape.489
  13.7 10.5 %all-to-all-start = ((bf16[32,2,256]{2,1,0:T(2,128)(2,1)}), bf16[32,2,256]{2,1,0:T(2,128)(2,1)S(1)}, u32[]{:S(2)}, u32[]{:S(2)}) async-start(bf16[32,2,256]{2,1,0:T(2,128)(2,1)} %reshape.489), calls=%async_computation | async-start | bytes 65536 | tf_op jit(solution)/shard_map/all_to_all | solution.py:39
  24.3 1.0 reduce-window.9
  25.7 0.3 convert_reduce_fusion.1
  26.0 4.5 gather_fusion.1
  30.6 2.3 gather_fusion.2
  32.9 6.8 gather_fusion.3
  40.0 0.6 convert_reduce_fusion.2
  40.8 78.1 %all-gather.5.cloned.1.call-done = bf16[16384,256]{1,0:T(8,128)(2,1)} async-done(((bf16[512,256]{1,0:T(8,128)(2,1)}), bf16[16384,256]{1,0:T(8,128)(2,1)}) %all-gather.5.cloned.1.call-update) | async-done | bytes 8388624 | tf_op jit(solution)/shard_map/all_gather | solution.py:62
  118.9 10.0 %gather_fusion.4 = bf16[128,128,256]{2,1,0:T(8,128)(2,1)} fusion(bf16[128,128,256]{2,1,0:T(8,128)(2,1)} %bitcast.161, s32[1024]{0:T(1024)S(1)} %pad_clamp_fusion), kind=kCustom, calls=%fused_computation.4 | custom fusion | bytes 16777728 | tf_op jit(solution)/shard_map/gather | solution.py:64
  128.9 7.7 convert_reduce_fusion
  136.6 0.6 multiply_convert_fusion.3
  137.3 0.8 fusion.72
  138.1 4.2 collective-permute-start
  142.4 1.9 collective-permute-start.1
  144.4 2.9 collective-permute-done.1
  147.3 0.9 fusion.49
  148.3 0.6 fusion.13
  148.9 58.6 %all-gather.7.cloned.1.call-done = bf16[32,16384]{1,0:T(8,128)(2,1)} async-done(((bf16[32,512]{1,0:T(8,128)(2,1)}), bf16[32,16384]{1,0:T(8,128)(2,1)}) %all-gather.7.cloned.1.call-update) | async-done | bytes 1048592 | tf_op jit(solution)/shard_map/all_gather | solution.py:95
  207.5 1.4 copy_bitcast_fusion.2
  208.9 0.8 gather_fusion.5
  209.7 2.9 fusion.3
  212.8 0.2 fusion.10
  212.9 102.0 %all-reduce = (f32[32]{0:T(128)S(1)}, f32[32]{0:T(128)S(1)}) all-reduce(f32[32]{0:T(128)S(1)} %get-tuple-element.6, f32[32]{0:T(128)S(1)} %get-tuple-element.5), channel_id=1, replica_groups=mesh['band'=32,'seq'=16] {'band','seq'}, use_global_device_ids=true, to_apply=%region_1.2 | all-reduce | flops 64 | bytes 512 | tf_op jit(solution)/shard_map/psum | solution.py:79
  315.0 0.2 multiply_reduce_fusion.2
  315.1 94.4 %psum.44 = f32[32]{0:T(128)S(1)} all-reduce(f32[32]{0:T(128)S(1)} %multiply_reduce_fusion.2), channel_id=1, replica_groups=mesh['band'=32,'seq'=16] {'band','seq'}, use_global_device_ids=true, to_apply=%region_10.11 | all-reduce | flops 32 | bytes 256 | tf_op jit(solution)/shard_map/psum | solution.py:79
  409.5 0.7 multiply_convert_fusion.2
  410.3 0.8 fusion.71
  411.1 3.1 collective-permute-start.2
  414.2 2.1 collective-permute-start.3
  416.3 2.9 collective-permute-done.3
  419.1 0.9 fusion.47
  420.1 0.6 fusion.14
  420.7 57.0 %all-gather.9.cloned.1.call-done = bf16[32,16384]{1,0:T(8,128)(2,1)} async-done(((bf16[32,512]{1,0:T(8,128)(2,1)}), bf16[32,16384]{1,0:T(8,128)(2,1)}) %all-gather.9.cloned.1.call-update) | async-done | bytes 1048592 | tf_op jit(solution)/shard_map/all_gather | solution.py:95
  477.7 1.4 copy_bitcast_fusion.1
  479.1 0.8 gather_fusion.6
  479.9 2.9 fusion.2
  482.8 0.1 copy.53
  482.9 0.2 multiply_reduce_fusion.1
  483.1 102.0 %psum.45 = f32[32]{0:T(128)S(1)} all-reduce(f32[32]{0:T(128)S(1)} %multiply_reduce_fusion.1), channel_id=1, replica_groups=mesh['band'=32,'seq'=16] {'band','seq'}, use_global_device_ids=true, to_apply=%region_12.13 | all-reduce | flops 32 | bytes 256 | tf_op jit(solution)/shard_map/psum | solution.py:101
  585.2 0.2 multiply_reduce_fusion
  585.4 94.4 %psum.46 = f32[32]{0:T(128)S(1)} all-reduce(f32[32]{0:T(128)S(1)} %multiply_reduce_fusion), channel_id=1, replica_groups=mesh['band'=32,'seq'=16] {'band','seq'}, use_global_device_ids=true, to_apply=%region_14.15 | all-reduce | flops 32 | bytes 256 | tf_op jit(solution)/shard_map/psum | solution.py:79
  679.8 0.7 multiply_convert_fusion.1
  680.5 0.8 fusion.70
  681.3 3.1 collective-permute-start.4
  684.4 1.9 collective-permute-start.5
  686.3 3.0 collective-permute-done.5
  689.3 0.9 fusion.45
  690.3 0.6 fusion.15
  690.9 57.1 %all-gather.11.cloned.1.call-done = bf16[32,16384]{1,0:T(8,128)(2,1)} async-done(((bf16[32,512]{1,0:T(8,128)(2,1)}), bf16[32,16384]{1,0:T(8,128)(2,1)}) %all-gather.11.cloned.1.call-update) | async-done | bytes 1048592 | tf_op jit(solution)/shard_map/all_gather | solution.py:95
  748.0 1.4 copy_bitcast_fusion
  749.4 0.8 gather_fusion.7
  750.1 2.9 fusion.1
  753.2 0.2 fusion.12
  753.5 102.0 %psum.47 = f32[32]{0:T(128)S(1)} all-reduce(f32[32]{0:T(128)S(1)} %fusion.12), channel_id=1, replica_groups=mesh['band'=32,'seq'=16] {'band','seq'}, use_global_device_ids=true, to_apply=%region_16.17 | all-reduce | flops 32 | bytes 256 | tf_op jit(solution)/shard_map/psum | solution.py:101
  855.5 0.7 multiply_add_fusion
  (54 shorter events, 1.7 us)
Async XLA Ops:
  6.5 33.2 %copy-start.1 = (s32[4,32]{1,0:T(4,128)S(1)}, s32[4,32]{1,0:T(4,128)}, u32[]{:S(2)}) copy-start(s32[4,32]{1,0:T(4,128)} %param.12) | copy-start | bytes 1540
  6.5 34.0 %copy-start.2 = (s32[4,32]{1,0:T(4,128)S(1)}, s32[4,32]{1,0:T(4,128)}, u32[]{:S(2)}) copy-start(s32[4,32]{1,0:T(4,128)} %param.13) | copy-start | bytes 1540
  6.5 112.4 %all-gather.5.cloned.1.call-start = ((), (), s32[]{:S(2)}) async-start(), calls=%async_computation.1 | async-start | bytes 8650752 | tf_op jit(solution)/shard_map/all_gather | solution.py:62
  13.7 26.9 %all-to-all-start = ((bf16[32,2,256]{2,1,0:T(2,128)(2,1)}), bf16[32,2,256]{2,1,0:T(2,128)(2,1)S(1)}, u32[]{:S(2)}, u32[]{:S(2)}) async-start(bf16[32,2,256]{2,1,0:T(2,128)(2,1)} %reshape.489), calls=%async_computation | async-start | bytes 65536 | tf_op jit(solution)/shard_map/all_to_all | solution.py:39
  24.3 183.2 %all-gather.7.cloned.1.call-start = ((), (), s32[]{:S(2)}) async-start(), calls=%async_computation.2 | async-start | bytes 1081344 | tf_op jit(solution)/shard_map/all_gather | solution.py:95
  118.9 10.0 %copy-start = (bf16[512,256]{1,0:T(8,128)(2,1)S(1)}, bf16[512,256]{1,0:T(8,128)(2,1)}, u32[]{:S(2)}) copy-start(bf16[512,256]{1,0:T(8,128)(2,1)} %param.11) | copy-start | bytes 786436
  137.3 340.4 %all-gather.9.cloned.1.call-start = ((), (), s32[]{:S(2)}) async-start(), calls=%async_computation.3 | async-start | bytes 1081344 | tf_op jit(solution)/shard_map/all_gather | solution.py:95
  138.1 6.3 collective-permute-start
  142.4 5.0 collective-permute-start.1
  410.2 337.7 %all-gather.11.cloned.1.call-start = ((), (), s32[]{:S(2)}) async-start(), calls=%async_computation.4 | async-start | bytes 1081344 | tf_op jit(solution)/shard_map/all_gather | solution.py:95
  411.1 5.2 collective-permute-start.2
  414.2 5.0 collective-permute-start.3
  681.3 5.0 collective-permute-start.4
  684.4 5.0 collective-permute-start.5
Sparse Core Ops, SparseCore 0:
  10.5 108.3 all-gather.4
  137.4 70.0 all-gather.6
  410.4 67.2 all-gather.8
  680.6 67.2 all-gather.10
where the time goes:
time: 864 us; the launch traced here: 863 us
  blocking collectives  495 us (57%)
  waiting for transfers between devices  260 us (30%)
  local copies, waits for them, and re-layouts  36.3 us (4%)
  starting transfers between devices  26.9 us (3%)
  matrix products  18.3 us (2%)
  between operations  13.5 us (2%)
  other arithmetic  12.5 us (1%)
    psum x3, blocking collectives, squares(): return lax.psum(jnp.sum(residual * residual, axis=1), ('band', 'seq'))  291 us
    psum x2, blocking collectives, on_device(): curve = lax.psum(jnp.sum(direction * image, axis=1), ('band', 'seq'))  204 us
    all_gather x3, waiting for transfers between devices, on_device(): lax.all_gather(lifted, 'band', axis=1, tiled=True)  173 us
    all_gather x1, waiting for transfers between devices, on_device(): gathered = lax.all_gather(embeddings, 'band', axis=0, tiled=True)  78.1 us
  transfers between devices with their start and end apart: 11, of which 7 were waited for; matrix products, arithmetic and copies ran while one was open for 3% of the time, Pallas kernels for 0%

commit v1 on v0

--- a/solution.py
+++ b/solution.py
@@ -76,7 +76,9 @@
     norm_scale = 1.0 / jnp.sqrt(near_degree + far_degree)
 
     def squares(residual):
-        return lax.psum(jnp.sum(residual * residual, axis=1), ("band", "seq"))
+        return jnp.sum(
+            lax.all_gather(jnp.sum(residual * residual, axis=1), ("band", "seq")), axis=0
+        )
 
     solution = jnp.zeros((channels, frames), jnp.float32)
     residual = labels

time: 864 us -> 1350 us (1.56)
  waiting for transfers between devices: 260 us -> 925 us
  blocking collectives: 495 us -> 307 us
    unnamed x4 -> x10, waiting for transfers between devices: 0.76 us -> 669 us
    psum x3 -> x0, blocking collectives: 291 us -> none  [squares(): return lax.psum(jnp.sum(residual * residual, axis=1), ('band', 'seq'))]
    psum x2 -> x3, blocking collectives: 204 us -> 307 us  [on_device(): curve = lax.psum(jnp.sum(direction * image, axis=1), ('band', 'seq'))]
  transfers between devices with their start and end apart: 11 -> 14, of which waited for: 7 -> 10; matrix products, arithmetic and copies ran while one was open for 3% -> 2% of each run, Pallas kernels for 0% -> 0%
where the time goes in v1:
time: 1350 us
  waiting for transfers between devices  925 us (69%)
  blocking collectives  307 us (23%)
  local copies, waits for them, and re-layouts  41.9 us (3%)
  starting transfers between devices  27.1 us (2%)
  matrix products  18.3 us (1%)
  between operations  13.9 us (1%)
    unnamed x10, waiting for transfers between devices  669 us
    psum x3, blocking collectives, on_device(): curve = lax.psum(jnp.sum(direction * image, axis=1), ('band', 'seq'))  307 us
    all_gather x3, waiting for transfers between devices, on_device(): lax.all_gather(lifted, 'band', axis=1, tiled=True)  168 us
    all_gather x1, waiting for transfers between devices, on_device(): gathered = lax.all_gather(embeddings, 'band', axis=0, tiled=True)  78.1 us
  transfers between devices with their start and end apart: 14, of which 10 were waited for; matrix products, arithmetic and copies ran while one was open for 2% of the time, Pallas kernels for 0%

profile of v1, /device:TPU:1, one launch (start us, length us, event | category | flops | bytes accessed | tf_op | source)
XLA Modules:
  0.0 1345.9 jit_solution(7462095712962470974)
XLA Ops:
  6.5 0.7 all-gather.8.cloned.1.call-update
  7.3 0.7 convert_element_type.47
  7.9 0.8 broadcast_multiply_fusion
  8.8 0.5 broadcast.327
  9.4 1.3 reduce.11
  10.8 0.7 compare_select_fusion.1
  11.5 1.3 gather_fusion
  13.0 0.8 reshape.508
  13.7 10.5 all-to-all-start
  24.3 1.0 reduce-window.9
  26.0 4.5 gather_fusion.1
  30.6 2.3 gather_fusion.2
  32.9 6.8 gather_fusion.3
  40.0 0.6 convert_reduce_fusion.2
  40.8 78.1 %all-gather.8.cloned.1.call-done = bf16[16384,256]{1,0:T(8,128)(2,1)} async-done(((bf16[512,256]{1,0:T(8,128)(2,1)}), bf16[16384,256]{1,0:T(8,128)(2,1)}) %all-gather.8.cloned.1.call-update) | async-done | bytes 8388624 | tf_op jit(solution)/shard_map/all_gather | solution.py:62
  118.9 10.0 gather_fusion.4
  128.9 7.7 convert_reduce_fusion
  136.6 0.6 multiply_convert_fusion.3
  137.3 0.8 fusion.72
  138.1 4.2 collective-permute-start
  142.4 1.9 collective-permute-start.1
  144.4 2.9 collective-permute-done.1
  147.3 0.9 fusion.49
  148.3 0.6 fusion.13
  148.9 58.6 %all-gather.10.cloned.1.call-done = bf16[32,16384]{1,0:T(8,128)(2,1)} async-done(((bf16[32,512]{1,0:T(8,128)(2,1)}), bf16[32,16384]{1,0:T(8,128)(2,1)}) %all-gather.10.cloned.1.call-update) | async-done | bytes 1048592 | tf_op jit(solution)/shard_map/all_gather | solution.py:97
  207.5 1.4 copy_bitcast_fusion.2
  208.9 0.8 gather_fusion.5
  209.7 2.9 fusion.3
  212.9 0.3 dynamic-update-slice
  213.2 0.6 copy-done.2
  213.9 103.2 %psum.21 = f32[32]{0:T(128)S(1)} all-reduce(f32[32]{0:T(128)S(1)} %get-tuple-element.5), channel_id=1, replica_groups=mesh['band'=32,'seq'=16] {'band','seq'}, use_global_device_ids=true, to_apply=%region_8.9 | all-reduce | flops 32 | bytes 256 | tf_op jit(solution)/shard_map/psum | solution.py:103
  317.0 159.8 %all-reduce.7.cloned.1.call-done = f32[16384]{0:T(1024)} async-done(((f32[16384]{0:T(1024)}), f32[16384]{0:T(1024)}) %all-reduce.7.cloned.1.call-update) | async-done | bytes 65552
  476.9 0.9 reshape.468
  478.4 0.6 copy-done.3
  479.1 254.7 %all-reduce.9.cloned.1.call-done = f32[16384]{0:T(1024)} async-done(((f32[16384]{0:T(1024)}), f32[16384]{0:T(1024)}) %all-reduce.9.cloned.1.call-update) | async-done | bytes 65552
  733.7 0.9 reshape.469
  734.8 0.7 multiply_convert_fusion.2
  735.6 0.8 fusion.71
  736.3 3.1 collective-permute-start.2
  739.4 2.1 collective-permute-start.3
  741.6 2.9 collective-permute-done.3
  744.4 0.9 fusion.47
  745.4 0.6 fusion.14
  745.9 54.6 %all-gather.12.cloned.1.call-done = bf16[32,16384]{1,0:T(8,128)(2,1)} async-done(((bf16[32,512]{1,0:T(8,128)(2,1)}), bf16[32,16384]{1,0:T(8,128)(2,1)}) %all-gather.12.cloned.1.call-update) | async-done | bytes 1048592 | tf_op jit(solution)/shard_map/all_gather | solution.py:97
  800.5 1.4 copy_bitcast_fusion.1
  801.9 0.8 gather_fusion.6
  802.7 2.9 fusion.2
  806.0 102.0 %psum.22 = f32[32]{0:T(128)S(1)} all-reduce(f32[32]{0:T(128)S(1)} %multiply_reduce_fusion.1), channel_id=1, replica_groups=mesh['band'=32,'seq'=16] {'band','seq'}, use_global_device_ids=true, to_apply=%region_12.13 | all-reduce | flops 32 | bytes 256 | tf_op jit(solution)/shard_map/psum | solution.py:103
  908.5 0.6 copy-done.1
  909.2 254.1 %all-reduce.11.cloned.1.call-done = f32[16384]{0:T(1024)} async-done(((f32[16384]{0:T(1024)}), f32[16384]{0:T(1024)}) %all-reduce.11.cloned.1.call-update) | async-done | bytes 65552
  1163.3 0.9 reshape.470
  1164.4 0.7 multiply_convert_fusion.1
  1165.1 0.8 fusion.70
  1165.9 3.1 collective-permute-start.4
  1169.0 1.9 collective-permute-start.5
  1171.0 3.0 collective-permute-done.5
  1174.0 0.9 fusion.45
  1174.9 0.6 fusion.15
  1175.5 55.2 %all-gather.14.cloned.1.call-done = bf16[32,16384]{1,0:T(8,128)(2,1)} async-done(((bf16[32,512]{1,0:T(8,128)(2,1)}), bf16[32,16384]{1,0:T(8,128)(2,1)}) %all-gather.14.cloned.1.call-update) | async-done | bytes 1048592 | tf_op jit(solution)/shard_map/all_gather | solution.py:97
  1230.7 1.4 copy_bitcast_fusion
  1232.2 0.8 gather_fusion.7
  1232.9 2.9 fusion.1
  1236.2 102.0 %psum.23 = f32[32]{0:T(128)S(1)} all-reduce(f32[32]{0:T(128)S(1)} %fusion.12), channel_id=1, replica_groups=mesh['band'=32,'seq'=16] {'band','seq'}, use_global_device_ids=true, to_apply=%region_16.17 | all-reduce | flops 32 | bytes 256 | tf_op jit(solution)/shard_map/psum | solution.py:103
  1338.3 0.7 multiply_add_fusion
  (79 shorter events, 4.2 us)
Async XLA Ops:
  6.5 33.2 %copy-start.4 = (s32[4,32]{1,0:T(4,128)S(1)}, s32[4,32]{1,0:T(4,128)}, u32[]{:S(2)}) copy-start(s32[4,32]{1,0:T(4,128)} %param.12) | copy-start | bytes 1540
  6.5 34.0 %copy-start.5 = (s32[4,32]{1,0:T(4,128)S(1)}, s32[4,32]{1,0:T(4,128)}, u32[]{:S(2)}) copy-start(s32[4,32]{1,0:T(4,128)} %param.13) | copy-start | bytes 1540
  6.5 112.4 %all-gather.8.cloned.1.call-start = ((), (), s32[]{:S(2)}) async-start(), calls=%async_computation.1 | async-start | bytes 8650752 | tf_op jit(solution)/shard_map/all_gather | solution.py:62
  13.7 26.8 %all-to-all-start = ((bf16[32,2,256]{2,1,0:T(2,128)(2,1)}), bf16[32,2,256]{2,1,0:T(2,128)(2,1)S(1)}, u32[]{:S(2)}, u32[]{:S(2)}) async-start(bf16[32,2,256]{2,1,0:T(2,128)(2,1)} %reshape.508), calls=%async_computation | async-start | bytes 65536 | tf_op jit(solution)/shard_map/all_to_all | solution.py:39
  24.3 183.2 %all-gather.10.cloned.1.call-start = ((), (), s32[]{:S(2)}) async-start(), calls=%async_computation.2 | async-start | bytes 1081344 | tf_op jit(solution)/shard_map/all_gather | solution.py:97
  118.9 10.0 copy-start
  137.3 339.6 %all-reduce.7.cloned.1.call-start = ((), (), s32[]{:S(2)}) async-start(), calls=%async_computation.5 | async-start | bytes 131072
  138.1 6.3 collective-permute-start
  142.4 5.0 collective-permute-start.1
  213.2 0.6 copy-start.2
  213.8 519.9 %all-reduce.9.cloned.1.call-start = ((), (), s32[]{:S(2)}) async-start(), calls=%async_computation.6 | async-start | bytes 131072
  478.4 0.6 copy-start.3
  479.0 321.5 %all-gather.12.cloned.1.call-start = ((), (), s32[]{:S(2)}) async-start(), calls=%async_computation.3 | async-start | bytes 1081344 | tf_op jit(solution)/shard_map/all_gather | solution.py:97
  735.5 427.8 %all-reduce.11.cloned.1.call-start = ((), (), s32[]{:S(2)}) async-start(), calls=%async_computation.7 | async-start | bytes 131072
  736.3 5.2 collective-permute-start.2
  739.4 5.0 collective-permute-start.3
  908.5 0.6 copy-start.1
  909.2 321.6 %all-gather.14.cloned.1.call-start = ((), (), s32[]{:S(2)}) async-start(), calls=%async_computation.4 | async-start | bytes 1081344 | tf_op jit(solution)/shard_map/all_gather | solution.py:97
  1165.9 5.0 collective-permute-start.4
  1169.0 5.0 collective-permute-start.5
Sparse Core Ops, SparseCore 0:
  10.5 108.3 all-gather.7
  137.4 70.0 all-gather.9
  214.0 262.8 all-reduce.6
  482.5 251.2 all-reduce.8
  736.6 63.8 all-gather.11
  909.3 254.0 all-reduce.10
  1166.8 63.8 all-gather.13
